TPU v7x, 32 devices: a whole 2x2x4 slice. The times are simulated.
32 devices in a mesh: dp: 4 (over z), fsdp: 2 (over x), rows: 4 (over y, core).
Axes of the slice: x: 2, y: 2, z: 4, core: 2. Of those that a mesh axis runs over, the one named last changes fastest.
Arguments:
- feature_maps: bfloat16 [8, 16, 32, 1536], P(('dp', 'fsdp'), 'rows'), may hold values from -30 to 30
- dw_kernel: float32 [7, 7, 1536], replicated, may hold values from -0.875 to 0.875
- norm_gain: float32 [1536], replicated, may hold values from 0.5 to 1.5
- w_up: bfloat16 [1536, 6144], P(('dp', 'rows'), 'fsdp'), may hold values from -0.15625 to 0.15625
- w_down: bfloat16 [6144, 1536], P('fsdp', ('dp', 'rows')), may hold values from -0.078125 to 0.078125
- layer_scale: float32 [1536], replicated, may hold values from 0.3 to 1.5
- d_out: bfloat16 [8, 16, 32, 1536], P(('dp', 'fsdp'), 'rows'), may hold values from -20 to 20
Outputs:
- result: bfloat16 [8, 16, 32, 1536], P(('dp', 'fsdp'), 'rows')
- grad_x: bfloat16 [8, 16, 32, 1536], P(('dp', 'fsdp'), 'rows')
- grad_up: float32 [1536, 6144], P(('dp', 'rows'), 'fsdp')
- grad_down: float32 [6144, 1536], P('fsdp', ('dp', 'rows'))
- grad_kernel: float32 [7, 7, 1536], replicated
- grad_gain: float32 [1536], replicated
- grad_scale: float32 [1536], replicated
All inputs are finite; a program needn't handle non-finite values.
Results may differ from a plain program's by a relative error of at most 0.0075.
Values may be sent and summed in bfloat16 or wider, within the bound.
No kernel may reach another device: no remote copies, remote signals or barrier semaphores. Data moves between devices by JAX's collectives and lax.ppermute only.
A program may use at most 128 MiB of HBM per device.

v0:
```python
import math
import jax
import jax.numpy as jnp
from jax import lax
from jax.sharding import PartitionSpec as P

KS = 7
norm_eps = 1e-06
inv_root_two = 1.0 / math.sqrt(2.0)
inv_root_two_pi = 1.0 / math.sqrt(2.0 * math.pi)
contract_rows = (((0,), (0,)), ((), ()))
contract_cols = (((1,), (1,)), ((), ()))


def padded_2(x, sides, width):
    for axis, dim in sides:
        devices, length = (lax.axis_size(axis), x.shape[dim])
        up = [(i, (i + 1) % devices) for i in range(devices - 1)]
        down = [(j, i) for i, j in up]
        last = lax.slice_in_dim(x, length - width, length, axis=dim)
        leading = lax.slice_in_dim(x, 0, width, axis=dim)
        before = lax.ppermute(last, axis, up)
        after = lax.ppermute(leading, axis, down)
        x = jnp.concatenate([before, x, after], axis=dim)
    return x


def gelu_exact(values):
    return 0.5 * values * (1.0 + jax.scipy.special.erf(values * inv_root_two))


def gelu_slope(values):
    cdf_part = 0.5 * (1.0 + jax.scipy.special.erf(values * inv_root_two))
    return cdf_part + values * jnp.exp(-0.5 * values * values) * inv_root_two_pi


def body(feature_maps, dw_kernel, norm_gain, w_up, w_down, layer_scale, d_out):
    scenes, strip, across, width = feature_maps.shape
    cells = scenes * strip * across
    hid_axes = ("fsdp", "rows")
    up_loc = lax.all_to_all(w_up, "rows", 1, 0, tiled=True)
    up_loc = lax.all_gather(up_loc, "dp", axis=0, tiled=True)
    down_loc = lax.all_to_all(w_down, "rows", 0, 1, tiled=True)
    down_loc = lax.all_gather(down_loc, "dp", axis=1, tiled=True)
    cotan = d_out.reshape(cells, width).astype(jnp.float32)
    back = (cotan * layer_scale).astype(jnp.bfloat16)
    back_all = lax.all_gather(back, hid_axes, axis=0, tiled=True)
    rimmed = padded_2(feature_maps, (("rows", 1),), 3)
    padded = jnp.pad(rimmed.astype(jnp.float32), ((0, 0), (0, 0), (3, 3), (0, 0)))
    filtered = jnp.zeros(feature_maps.shape, jnp.float32)
    for row_off in range(KS):
        for col_off in range(KS):
            filtered = (
                filtered
                + padded[:, row_off : row_off + strip, col_off : col_off + across, :]
                * dw_kernel[row_off, col_off]
            )
    flat = filtered.reshape(cells, width)
    average = jnp.mean(flat, axis=-1, keepdims=True)
    center = flat - average
    variance = jnp.mean(center * center, axis=-1, keepdims=True)
    rstd = lax.rsqrt(variance + norm_eps)
    normed = center * rstd
    scaled = (normed * norm_gain).astype(jnp.bfloat16)
    gathered = lax.all_gather(scaled, hid_axes, axis=0, tiled=True)
    hidden = jnp.dot(gathered, up_loc, preferred_element_type=jnp.float32)
    active = gelu_exact(hidden).astype(jnp.bfloat16)
    mlp_terms = jnp.dot(active, down_loc, preferred_element_type=jnp.float32)
    branch = lax.psum_scatter(
        mlp_terms.astype(jnp.bfloat16), hid_axes, scatter_dimension=0, tiled=True
    ).astype(jnp.float32)
    resid = feature_maps.reshape(cells, width).astype(jnp.float32)
    result = (resid + layer_scale * branch).astype(jnp.bfloat16).reshape(feature_maps.shape)
    scale_part = jnp.sum(cotan * branch, axis=0)
    down_part = lax.dot_general(active, back_all, contract_rows, preferred_element_type=jnp.float32)
    slope_in = lax.dot_general(
        back_all, down_loc, contract_cols, preferred_element_type=jnp.float32
    )
    hidden_grad = (slope_in * gelu_slope(hidden)).astype(jnp.bfloat16)
    up_part = lax.dot_general(
        gathered, hidden_grad, contract_rows, preferred_element_type=jnp.float32
    )
    norm_terms = lax.dot_general(
        hidden_grad, up_loc, contract_cols, preferred_element_type=jnp.float32
    )
    norm_grad = lax.psum_scatter(norm_terms, hid_axes, scatter_dimension=0, tiled=True)
    grad_up = lax.psum_scatter(up_part, "dp", scatter_dimension=0, tiled=True)
    grad_up = lax.all_to_all(grad_up, "rows", 0, 1, tiled=True)
    grad_down = lax.psum_scatter(down_part, "dp", scatter_dimension=1, tiled=True)
    grad_down = lax.all_to_all(grad_down, "rows", 1, 0, tiled=True)
    gain_part = jnp.sum(norm_grad * normed, axis=0)
    scaled_grad = norm_grad * norm_gain
    conv_grad = rstd * (
        scaled_grad
        - jnp.mean(scaled_grad, axis=-1, keepdims=True)
        - normed * jnp.mean(scaled_grad * normed, axis=-1, keepdims=True)
    )
    conv_grad = conv_grad.reshape(feature_maps.shape)
    grad_rim = padded_2(conv_grad.astype(jnp.bfloat16), (("rows", 1),), 3).astype(conv_grad.dtype)
    grad_pad = jnp.pad(grad_rim, ((0, 0), (0, 0), (3, 3), (0, 0)))
    kernel_rows = []
    back_conv = jnp.zeros(feature_maps.shape, jnp.float32)
    for row_off in range(KS):
        for col_off in range(KS):
            window = padded[:, row_off : row_off + strip, col_off : col_off + across, :]
            kernel_rows.append(jnp.sum(window * conv_grad, axis=(0, 1, 2)))
            back_conv = (
                back_conv
                + grad_pad[
                    :, 6 - row_off : 6 - row_off + strip, 6 - col_off : 6 - col_off + across, :
                ]
                * dw_kernel[row_off, col_off]
            )
    kernel_part = jnp.stack(kernel_rows).reshape(KS, KS, width)
    grad_x = (d_out.astype(jnp.float32) + back_conv).astype(jnp.bfloat16)
    grad_kernel, grad_gain, grad_scale = lax.psum(
        (kernel_part, gain_part, scale_part), ("dp", "fsdp", "rows")
    )
    return (result, grad_x, grad_up, grad_down, grad_kernel, grad_gain, grad_scale)


def solution(mesh):
    return jax.shard_map(
        body,
        mesh=mesh,
        in_specs=(
            P(("dp", "fsdp"), "rows", None, None),
            P(),
            P(),
            P(("dp", "rows"), "fsdp"),
            P("fsdp", ("dp", "rows")),
            P(),
            P(("dp", "fsdp"), "rows", None, None),
        ),
        out_specs=(
            P(("dp", "fsdp"), "rows", None, None),
            P(("dp", "fsdp"), "rows", None, None),
            P(("dp", "rows"), "fsdp"),
            P("fsdp", ("dp", "rows")),
            P(),
            P(),
            P(),
        ),
        check_vma=False,
    )
```

profile of v0, /device:TPU:1, one launch (start us, length us, event | category | flops | bytes accessed | tf_op | source)
XLA Modules:
  0.0 634.2 jit_solution(6933835637550639418)
XLA Ops:
  7.2 1.2 copy.35
  8.4 13.0 %all_to_all.76 = bf16[96,4,768]{2,0,1:T(8,128)(2,1)} all-to-all(bf16[96,4,768]{2,0,1:T(8,128)(2,1)S(1)} %bitcast.112), channel_id=1, replica_groups=mesh['dp'=4,'fsdp'=2,'rows'=4] {'rows'}, dimensions={1} | all-to-all | bytes 1179648 | tf_op jit(solution)/shard_map/all_to_all | solution.py:41
  21.5 2.6 collective-permute-start
  24.2 1.9 collective-permute-start.1
  26.9 0.9 slice_reduce_fusion.47
  27.9 4.3 collective-permute-done.1
  32.4 9.5 %fusion.103 = (f32[4,32]{1,0:T(4,128)S(1)}, f32[1,4,32,1536]{3,2,1,0:T(8,128)S(1)}) fusion(f32[1536]{0:T(1024)S(1)} %get-tuple-element.106, f32[1536]{0:T(1024)S(1)} %get-tuple-element.107, f32[1536]{0:T(1024)S(1)} %get-tuple-element.60, f32[1536]{0:T(1024)S(1)} %get-tuple-element.61, f32[1,10,32,1536]{3,2,1,0:T(8,128)S(1)} %maximum_convert_fusion, ...), kind=kLoop, calls=%fused_computation.315 | loop fusion | flops 19267456 | bytes 8641024 | tf_op jit(solution)/shard_map/reduce_sum | solution.py:59
  42.6 0.9 multiply_convert_fusion.1
  43.6 1.1 copy.34
  44.7 10.7 %all_to_all.77 = bf16[4,768,96]{1,2,0:T(8,128)(2,1)} all-to-all(bf16[4,768,96]{1,2,0:T(8,128)(2,1)S(1)} %bitcast.113), channel_id=1, replica_groups=mesh['dp'=4,'fsdp'=2,'rows'=4] {'rows'}, dimensions={0} | all-to-all | bytes 1179648 | tf_op jit(solution)/shard_map/all_to_all | solution.py:43
  55.5 17.3 %all-gather.7.cloned.1.call-done = bf16[1536,768]{1,0:T(8,128)(2,1)} async-done(((bf16[384,768]{1,0:T(8,128)(2,1)}), bf16[1536,768]{1,0:T(8,128)(2,1)}) %all-gather.7.cloned.1.call-update) | async-done | bytes 2359312 | tf_op jit(solution)/shard_map/all_gather | solution.py:42
  72.8 34.1 %all-gather.5.cloned.1.call-done = bf16[1024,1536]{1,0:T(8,128)(2,1)} async-done(((bf16[128,1536]{1,0:T(8,128)(2,1)}), bf16[1024,1536]{1,0:T(8,128)(2,1)}) %all-gather.5.cloned.1.call-update) | async-done | bytes 3145744 | tf_op jit(solution)/shard_map/all_gather | solution.py:65
  106.9 7.4 %multiply_convert_fusion = (bf16[1024,768]{1,0:T(8,128)(2,1)}, f32[1024,768]{1,0:T(8,128)}) fusion(bf16[1024,1536]{1,0:T(8,128)(2,1)} %all-gather.5.cloned.1.call-done, bf16[1536,768]{1,0:T(8,128)(2,1)} %all-gather.7.cloned.1.call-done), kind=kOutput, calls=%fused_computation.92 | convolution fusion | flops 2419851264 | bytes 10223616 | tf_op jit(solution)/shard_map/dot_general | solution.py:66
  114.3 44.2 %all-gather.9.cloned.1.call-done = bf16[768,1536]{0,1:T(8,128)(2,1)} async-done(((bf16[768,384]{0,1:T(8,128)(2,1)}), bf16[768,1536]{0,1:T(8,128)(2,1)}) %all-gather.9.cloned.1.call-update) | async-done | bytes 2359312 | tf_op jit(solution)/shard_map/all_gather | solution.py:44
  158.5 6.5 %convolution_convert_fusion = bf16[1024,1536]{1,0:T(8,128)(2,1)} fusion(bf16[1024,768]{1,0:T(8,128)(2,1)} %get-tuple-element.120, bf16[768,1536]{0,1:T(8,128)(2,1)} %all-gather.9.cloned.1.call-done), kind=kOutput, calls=%fused_computation.85 | convolution fusion | flops 2417491968 | bytes 7077888 | tf_op jit(solution)/shard_map/dot_general | solution.py:68
  165.1 45.2 %reduce-scatter.5.cloned.1.call-done = bf16[128,1536]{1,0:T(8,128)(2,1)} async-done(((bf16[1024,1536]{1,0:T(8,128)(2,1)}), bf16[128,1536]{1,0:T(8,128)(2,1)}) %reduce-scatter.5.cloned.1.call-update) | async-done | bytes 393232 | tf_op jit(solution)/shard_map/reduce_scatter | solution.py:69
  210.2 2.7 fusion.8
  213.2 32.7 %all-gather.11.cloned.1.call-done = bf16[1024,1536]{1,0:T(8,128)(2,1)} async-done(((bf16[128,1536]{1,0:T(8,128)(2,1)}), bf16[1024,1536]{1,0:T(8,128)(2,1)}) %all-gather.11.cloned.1.call-update) | async-done | bytes 3145744 | tf_op jit(solution)/shard_map/all_gather | solution.py:47
  245.9 7.2 %fusion.108 = f32[768,1536]{1,0:T(8,128)} fusion(bf16[1024,768]{1,0:T(8,128)(2,1)} %get-tuple-element.120, bf16[1024,1536]{1,0:T(8,128)(2,1)} %all-gather.11.cloned.1.call-done), kind=kOutput, calls=%fused_computation.320 | convolution fusion | flops 2415919104 | bytes 9437184 | tf_op jit(solution)/shard_map/dot_general | solution.py:75
  253.1 6.8 %fusion.5 = bf16[1024,768]{1,0:T(8,128)(2,1)S(1)} fusion(f32[1024,768]{1,0:T(8,128)} %get-tuple-element.121, bf16[1024,1536]{1,0:T(8,128)(2,1)} %all-gather.11.cloned.1.call-done, bf16[768,1536]{0,1:T(8,128)(2,1)} %all-gather.9.cloned.1.call-done), kind=kOutput, calls=%fused_computation.91 | convolution fusion | flops 2423783424 | bytes 10223616 | tf_op jit(solution)/shard_map/dot_general | solution.py:76
  260.0 1.2 copy-done.49
  261.1 4.6 fusion.106
  265.8 7.2 %fusion.107 = f32[1536,768]{1,0:T(8,128)} fusion(bf16[1024,1536]{1,0:T(8,128)(2,1)} %all-gather.5.cloned.1.call-done, bf16[1024,768]{1,0:T(8,128)(2,1)} %copy-done.49), kind=kOutput, calls=%fused_computation.319 | convolution fusion | flops 2415919104 | bytes 9437184 | tf_op jit(solution)/shard_map/dot_general | solution.py:80
  273.0 65.1 %reduce-scatter.11.cloned.1.call-done = f32[768,384]{1,0:T(8,128)} async-done(((f32[768,1536]{1,0:T(8,128)}), f32[768,384]{1,0:T(8,128)}) %reduce-scatter.11.cloned.1.call-update) | async-done | bytes 1179664 | tf_op jit(solution)/shard_map/reduce_scatter | solution.py:89
  338.1 2.7 copy.26
  340.8 4.9 all-to-all-start.3
  345.7 58.4 %reduce-scatter.7.cloned.1.call-done = f32[128,1536]{1,0:T(8,128)} async-done(((f32[1024,1536]{1,0:T(8,128)}), f32[128,1536]{1,0:T(8,128)}) %reduce-scatter.7.cloned.1.call-update) | async-done | bytes 786448 | tf_op jit(solution)/shard_map/reduce_scatter | solution.py:86
  404.1 2.0 multiply_reduce_fusion
  406.2 3.6 multiply_reduce_fusion.2
  409.8 2.0 multiply_reduce_fusion.1
  411.8 0.9 fusion.104
  414.5 0.6 stack.172
  416.3 0.6 stack.176
  420.5 0.6 stack.184
  424.1 3.6 collective-permute-start.2
  427.7 1.9 collective-permute-start.3
  429.6 1.1 multiply_reduce_fusion.3
  431.2 4.2 stack.199
  435.4 0.8 reshape.335
  436.2 46.1 %all-reduce.2 = (f32[1536]{0:T(1024)}, f32[1536]{0:T(1024)}) all-reduce(f32[1536]{0:T(1024)} %get-tuple-element.56, f32[1536]{0:T(1024)} %get-tuple-element.113), channel_id=1, replica_groups=mesh['dp'=4,'fsdp'=2,'rows'=4] {'dp','fsdp','rows'}, use_global_device_ids=true, to_apply=%region_59.60 | all-reduce | flops 3072 | bytes 24576 | tf_op jit(solution)/shard_map/psum | solution.py:116
  482.4 10.4 %reduce-scatter.9.cloned.1.call-done = f32[384,768]{1,0:T(8,128)} async-done(((f32[1536,768]{1,0:T(8,128)}), f32[384,768]{1,0:T(8,128)}) %reduce-scatter.9.cloned.1.call-update) | async-done | bytes 1179664 | tf_op jit(solution)/shard_map/reduce_scatter | solution.py:87
  492.8 4.1 all-to-all-start.2
  496.9 8.0 %fusion.96 = bf16[1,4,32,1536]{3,2,1,0:T(8,128)(2,1)} fusion(f32[1,10,32,1536]{3,2,1,0:T(8,128)S(1)} %maximum_convert_fusion.1, bf16[1,4,32,1536]{3,2,1,0:T(8,128)(2,1)S(1)} %copy-done.1, f32[1536]{0:T(1024)} %copy-done.13, f32[1536]{0:T(1024)} %copy-done.14, f32[1536]{0:T(1024)} %copy-done.16, f32[1536]{0:T(1024)} %copy-done.17, f32[1536]{0:T(1024)} %copy-done.18, ...), kind=kLoop, calls=%fused_computation.188 | loop fusion | flops 19660800 | bytes 8562688 | tf_op jit(solution)/shard_map/convert_element_type | solution.py:115
  504.9 2.4 copy.31
  507.3 5.2 all-to-all-done.2
  512.5 1.1 copy.30
  513.7 112.3 %all-reduce.5.cloned.1.call-done = f32[7,7,1536]{2,1,0:T(8,128)} async-done(((f32[7,7,1536]{2,1,0:T(8,128)}), f32[7,7,1536]{2,1,0:T(8,128)}) %all-reduce.5.cloned.1.call-update) | async-done | bytes 301072 | tf_op jit(solution)/shard_map/psum | solution.py:116
  626.0 1.7 copy.37
  (180 shorter events, 11.9 us)
Async XLA Ops:
  7.2 18.9 %copy-start.2 = (f32[7,7,1536]{2,1,0:T(8,128)S(1)}, f32[7,7,1536]{2,1,0:T(8,128)}, u32[]{:S(2)}) copy-start(f32[7,7,1536]{2,1,0:T(8,128)} %param.8) | copy-start | bytes 903172
  7.2 65.6 %all-gather.7.cloned.1.call-start = ((), (), s32[]{:S(2)}) async-start(), calls=%async_computation.9 | async-start | bytes 2949120 | tf_op jit(solution)/shard_map/all_gather | solution.py:42
  21.4 85.5 %all-gather.5.cloned.1.call-start = ((), (), s32[]{:S(2)}) async-start(), calls=%async_computation.8 | async-start | bytes 3538944 | tf_op jit(solution)/shard_map/all_gather | solution.py:65
  21.5 6.3 %collective-permute-start = (bf16[1,3,32,1536]{3,2,1,0:T(8,128)(2,1)S(1)}, bf16[1,3,32,1536]{3,2,1,0:T(8,128)(2,1)S(1)}, u32[]{:S(2)}, u32[]{:S(2)}) collective-permute-start(bf16[1,3,32,1536]{3,2,1,0:T(8,128)(2,1)S(1)} %get-tuple-element.118), channel_id=1, source_target_pairs={{0,1},{1,2},{2,3},{4,5},{5,6},{6,7},{8,9},{9,10},{10,11},{12,13},{... | collective-permute-start | bytes 884744 | tf_op jit(solution)/shard_map/ppermute | solution.py:22
  24.2 8.0 %collective-permute-start.1 = (bf16[1,3,32,1536]{3,2,1,0:T(8,128)(2,1)S(1)}, bf16[1,3,32,1536]{3,2,1,0:T(8,128)(2,1)S(1)}, u32[]{:S(2)}, u32[]{:S(2)}) collective-permute-start(bf16[1,3,32,1536]{3,2,1,0:T(8,128)(2,1)S(1)} %get-tuple-element.119), channel_id=1, source_target_pairs={{1,0},{2,1},{3,2},{5,4},{6,5},{7,6},{9,8},{10,9},{11,10},{13,12},{... | collective-permute-start | bytes 884744 | tf_op jit(solution)/shard_map/ppermute | solution.py:23
  26.3 15.5 %copy-start.4 = (f32[1536]{0:T(1024)}, f32[1536]{0:T(1024)S(1)}, u32[]{:S(2)}) copy-start(f32[1536]{0:T(1024)S(1)} %get-tuple-element.98) | copy-start | bytes 18436
  26.3 15.5 %copy-start.6 = (f32[1536]{0:T(1024)}, f32[1536]{0:T(1024)S(1)}, u32[]{:S(2)}) copy-start(f32[1536]{0:T(1024)S(1)} %get-tuple-element.99) | copy-start | bytes 18436
  26.3 15.5 %copy-start.7 = (f32[1536]{0:T(1024)}, f32[1536]{0:T(1024)S(1)}, u32[]{:S(2)}) copy-start(f32[1536]{0:T(1024)S(1)} %get-tuple-element.100) | copy-start | bytes 18436
  26.3 15.5 %copy-start.8 = (f32[1536]{0:T(1024)}, f32[1536]{0:T(1024)S(1)}, u32[]{:S(2)}) copy-start(f32[1536]{0:T(1024)S(1)} %get-tuple-element.101) | copy-start | bytes 18436
  26.3 15.5 %copy-start.9 = (f32[1536]{0:T(1024)}, f32[1536]{0:T(1024)S(1)}, u32[]{:S(2)}) copy-start(f32[1536]{0:T(1024)S(1)} %get-tuple-element.102) | copy-start | bytes 18436
  26.3 15.5 %copy-start.10 = (f32[1536]{0:T(1024)}, f32[1536]{0:T(1024)S(1)}, u32[]{:S(2)}) copy-start(f32[1536]{0:T(1024)S(1)} %get-tuple-element.103) | copy-start | bytes 18436
  26.4 15.5 %copy-start.11 = (f32[1536]{0:T(1024)}, f32[1536]{0:T(1024)S(1)}, u32[]{:S(2)}) copy-start(f32[1536]{0:T(1024)S(1)} %get-tuple-element.104) | copy-start | bytes 18436
  26.4 15.5 %copy-start.12 = (f32[1536]{0:T(1024)}, f32[1536]{0:T(1024)S(1)}, u32[]{:S(2)}) copy-start(f32[1536]{0:T(1024)S(1)} %get-tuple-element.105) | copy-start | bytes 18436
  26.4 15.5 %copy-start.13 = (f32[1536]{0:T(1024)}, f32[1536]{0:T(1024)S(1)}, u32[]{:S(2)}) copy-start(f32[1536]{0:T(1024)S(1)} %get-tuple-element.106) | copy-start | bytes 18436
  26.4 15.5 %copy-start.14 = (f32[1536]{0:T(1024)}, f32[1536]{0:T(1024)S(1)}, u32[]{:S(2)}) copy-start(f32[1536]{0:T(1024)S(1)} %get-tuple-element.107) | copy-start | bytes 18436
  26.7 15.2 %copy-start.15 = (f32[1536]{0:T(1024)}, f32[1536]{0:T(1024)S(1)}, u32[]{:S(2)}) copy-start(f32[1536]{0:T(1024)S(1)} %get-tuple-element.59) | copy-start | bytes 18436
  26.7 15.2 %copy-start.16 = (f32[1536]{0:T(1024)}, f32[1536]{0:T(1024)S(1)}, u32[]{:S(2)}) copy-start(f32[1536]{0:T(1024)S(1)} %get-tuple-element.60) | copy-start | bytes 18436
  26.7 15.2 %copy-start.17 = (f32[1536]{0:T(1024)}, f32[1536]{0:T(1024)S(1)}, u32[]{:S(2)}) copy-start(f32[1536]{0:T(1024)S(1)} %get-tuple-element.61) | copy-start | bytes 18436
  26.7 15.2 %copy-start.18 = (f32[1536]{0:T(1024)}, f32[1536]{0:T(1024)S(1)}, u32[]{:S(2)}) copy-start(f32[1536]{0:T(1024)S(1)} %get-tuple-element.62) | copy-start | bytes 18436
  26.8 15.2 %copy-start.19 = (f32[1536]{0:T(1024)}, f32[1536]{0:T(1024)S(1)}, u32[]{:S(2)}) copy-start(f32[1536]{0:T(1024)S(1)} %get-tuple-element.63) | copy-start | bytes 18436
  26.8 15.2 %copy-start.20 = (f32[1536]{0:T(1024)}, f32[1536]{0:T(1024)S(1)}, u32[]{:S(2)}) copy-start(f32[1536]{0:T(1024)S(1)} %get-tuple-element.64) | copy-start | bytes 18436
  26.8 15.2 %copy-start.21 = (f32[1536]{0:T(1024)}, f32[1536]{0:T(1024)S(1)}, u32[]{:S(2)}) copy-start(f32[1536]{0:T(1024)S(1)} %get-tuple-element.65) | copy-start | bytes 18436
  26.8 15.2 %copy-start.22 = (f32[1536]{0:T(1024)}, f32[1536]{0:T(1024)S(1)}, u32[]{:S(2)}) copy-start(f32[1536]{0:T(1024)S(1)} %get-tuple-element.66) | copy-start | bytes 18436
  26.8 15.2 %copy-start.23 = (f32[1536]{0:T(1024)}, f32[1536]{0:T(1024)S(1)}, u32[]{:S(2)}) copy-start(f32[1536]{0:T(1024)S(1)} %get-tuple-element.67) | copy-start | bytes 18436
  26.8 15.2 %copy-start.24 = (f32[1536]{0:T(1024)}, f32[1536]{0:T(1024)S(1)}, u32[]{:S(2)}) copy-start(f32[1536]{0:T(1024)S(1)} %get-tuple-element.68) | copy-start | bytes 18436
  26.8 15.2 %copy-start.25 = (f32[1536]{0:T(1024)}, f32[1536]{0:T(1024)S(1)}, u32[]{:S(2)}) copy-start(f32[1536]{0:T(1024)S(1)} %get-tuple-element.69) | copy-start | bytes 18436
  26.8 15.2 %copy-start.26 = (f32[1536]{0:T(1024)}, f32[1536]{0:T(1024)S(1)}, u32[]{:S(2)}) copy-start(f32[1536]{0:T(1024)S(1)} %get-tuple-element.70) | copy-start | bytes 18436
  26.8 15.2 %copy-start.27 = (f32[1536]{0:T(1024)}, f32[1536]{0:T(1024)S(1)}, u32[]{:S(2)}) copy-start(f32[1536]{0:T(1024)S(1)} %get-tuple-element.71) | copy-start | bytes 18436
  26.8 15.2 %copy-start.28 = (f32[1536]{0:T(1024)}, f32[1536]{0:T(1024)S(1)}, u32[]{:S(2)}) copy-start(f32[1536]{0:T(1024)S(1)} %get-tuple-element.72) | copy-start | bytes 18436
  26.9 15.2 %copy-start.29 = (f32[1536]{0:T(1024)}, f32[1536]{0:T(1024)S(1)}, u32[]{:S(2)}) copy-start(f32[1536]{0:T(1024)S(1)} %get-tuple-element.73) | copy-start | bytes 18436
  26.9 15.2 %copy-start.30 = (f32[1536]{0:T(1024)}, f32[1536]{0:T(1024)S(1)}, u32[]{:S(2)}) copy-start(f32[1536]{0:T(1024)S(1)} %get-tuple-element.74) | copy-start | bytes 18436
  26.9 15.2 %copy-start.31 = (f32[1536]{0:T(1024)}, f32[1536]{0:T(1024)S(1)}, u32[]{:S(2)}) copy-start(f32[1536]{0:T(1024)S(1)} %get-tuple-element.75) | copy-start | bytes 18436
  26.9 15.2 %copy-start.32 = (f32[1536]{0:T(1024)}, f32[1536]{0:T(1024)S(1)}, u32[]{:S(2)}) copy-start(f32[1536]{0:T(1024)S(1)} %get-tuple-element.76) | copy-start | bytes 18436
  42.6 71.7 %copy-start.46 = (f32[128]{0:T(128)}, f32[128]{0:T(128)S(1)}, u32[]{:S(2)}) copy-start(f32[128]{0:T(128)S(1)} %rsqrt.12) | copy-start | bytes 1540
  43.6 114.9 %all-gather.9.cloned.1.call-start = ((), (), s32[]{:S(2)}) async-start(), calls=%async_computation.10 | async-start | bytes 2949120 | tf_op jit(solution)/shard_map/all_gather | solution.py:44
  55.4 154.8 %reduce-scatter.5.cloned.1.call-start = ((), (), s32[]{:S(2)}) async-start(), calls=%async_computation.11 | async-start | bytes 3538944 | tf_op jit(solution)/shard_map/reduce_scatter | solution.py:69
  165.0 45.2 %copy-start.1 = (bf16[1,4,32,1536]{3,2,1,0:T(8,128)(2,1)S(1)}, bf16[1,4,32,1536]{3,2,1,0:T(8,128)(2,1)}, u32[]{:S(2)}) copy-start(bf16[1,4,32,1536]{3,2,1,0:T(8,128)(2,1)} %param.13) | copy-start | bytes 1179652
  165.0 80.8 %all-gather.11.cloned.1.call-start = ((), (), s32[]{:S(2)}) async-start(), calls=%async_computation.12 | async-start | bytes 3538944 | tf_op jit(solution)/shard_map/all_gather | solution.py:47
  213.0 125.2 %reduce-scatter.11.cloned.1.call-start = ((), (), s32[]{:S(2)}) async-start(), calls=%async_computation.15 | async-start | bytes 5898240 | tf_op jit(solution)/shard_map/reduce_scatter | solution.py:89
  253.1 151.0 %reduce-scatter.7.cloned.1.call-start = ((), (), s32[]{:S(2)}) async-start(), calls=%async_computation.13 | async-start | bytes 7077888 | tf_op jit(solution)/shard_map/reduce_scatter | solution.py:86
  265.7 227.1 %reduce-scatter.9.cloned.1.call-start = ((), (), s32[]{:S(2)}) async-start(), calls=%async_computation.14 | async-start | bytes 5898240 | tf_op jit(solution)/shard_map/reduce_scatter | solution.py:87
  273.0 131.1 %copy-start.45 = (f32[128]{0:T(128)S(1)}, f32[128]{0:T(128)}, u32[]{:S(2)}) copy-start(f32[128]{0:T(128)} %copy-done.44) | copy-start | bytes 1540
  273.0 131.1 %copy-start.47 = (f32[128]{0:T(128)S(1)}, f32[128]{0:T(128)}, u32[]{:S(2)}) copy-start(f32[128]{0:T(128)} %copy-done.46) | copy-start | bytes 1540
  340.8 152.0 %all-to-all-start.3 = ((f32[768,4,96]{0,2,1:T(8,128)}), f32[768,4,96]{0,2,1:T(8,128)}, u32[]{:S(2)}, u32[]{:S(2)}) async-start(f32[768,4,96]{0,2,1:T(8,128)} %bitcast.108), calls=%async_computation.7 | async-start | bytes 2359296 | tf_op jit(solution)/shard_map/all_to_all | solution.py:90
  345.7 280.3 %all-reduce.5.cloned.1.call-start = ((), (), s32[]{:S(2)}) async-start(), calls=%async_computation.16 | async-start | bytes 688128 | tf_op jit(solution)/shard_map/psum | solution.py:116
  424.1 58.2 %collective-permute-start.2 = (bf16[1,3,32,1536]{3,2,1,0:T(8,128)(2,1)}, bf16[1,3,32,1536]{3,2,1,0:T(8,128)(2,1)S(1)}, u32[]{:S(2)}, u32[]{:S(2)}) collective-permute-start(bf16[1,3,32,1536]{3,2,1,0:T(8,128)(2,1)} %get-tuple-element.116), channel_id=1, source_target_pairs={{0,1},{1,2},{2,3},{4,5},{5,6},{6,7},{8,9},{9,10},{10,11},{12,13},{... | collective-permute-start | bytes 884744 | tf_op jit(solution)/shard_map/ppermute | solution.py:22
  427.7 54.6 %collective-permute-start.3 = (bf16[1,3,32,1536]{3,2,1,0:T(8,128)(2,1)}, bf16[1,3,32,1536]{3,2,1,0:T(8,128)(2,1)S(1)}, u32[]{:S(2)}, u32[]{:S(2)}) collective-permute-start(bf16[1,3,32,1536]{3,2,1,0:T(8,128)(2,1)} %get-tuple-element.117), channel_id=1, source_target_pairs={{1,0},{2,1},{3,2},{5,4},{6,5},{7,6},{9,8},{10,9},{11,10},{13,12},{... | collective-permute-start | bytes 884744 | tf_op jit(solution)/shard_map/ppermute | solution.py:23
  492.8 19.8 %all-to-all-start.2 = ((f32[4,96,768]{2,1,0:T(8,128)}), f32[4,96,768]{2,1,0:T(8,128)S(1)}, u32[]{:S(2)}, u32[]{:S(2)}) async-start(f32[4,96,768]{2,1,0:T(8,128)} %bitcast.115), calls=%async_computation.5 | async-start | bytes 2359296 | tf_op jit(solution)/shard_map/all_to_all | solution.py:88
  (17 other events, 220.0 us)
Sparse Core Ops, SparseCore 0:
  21.5 51.2 all-gather.6
  75.3 31.5 all-gather.4
  108.5 50.0 all-gather.8
  165.1 45.0 reduce-scatter.4
  213.1 32.7 all-gather.10
  253.2 84.8 reduce-scatter.10
  341.9 62.1 reduce-scatter.6
  406.4 86.3 reduce-scatter.8
  498.7 127.2 all-reduce.4
where the time goes:
time: 635 us; the launch traced here: 634 us
  waiting for transfers between devices  429 us (68%)
  blocking collectives  69.8 us (11%)
  matrix products  39.7 us (6%)
  local copies, waits for them, and re-layouts  30.5 us (5%)
  other arithmetic  30.4 us (5%)
  starting transfers between devices  19.6 us (3%)
  between operations  14.9 us (2%)
    psum x1, waiting for transfers between devices, body(): lax.psum((kernel_part, gain_part, scale_part), ('dp', 'fsdp', 'rows'))  112 us
    reduce_scatter x1, waiting for transfers between devices, body(): lax.psum_scatter(down_part, 'dp', scatter_dimension=1, tiled=True)  65.1 us
    reduce_scatter x1, waiting for transfers between devices, body(): lax.psum_scatter(norm_terms, hid_axes, scatter_dimension=0, tiled=True)  58.4 us
    psum x1, blocking collectives, body(): lax.psum((kernel_part, gain_part, scale_part), ('dp', 'fsdp', 'rows'))  46.1 us
    reduce_scatter x1, waiting for transfers between devices, body(): lax.psum_scatter(mlp_terms.astype(jnp.bfloat16), hid_axes, scatter_dimens...  45.2 us
    all_gather x1, waiting for transfers between devices, body(): down_loc = lax.all_gather(down_loc, 'dp', axis=1, tiled=True)  44.2 us
    all_gather x1, waiting for transfers between devices, body(): gathered = lax.all_gather(scaled, hid_axes, axis=0, tiled=True)  34.1 us
    all_gather x1, waiting for transfers between devices, body(): back_all = lax.all_gather(back, hid_axes, axis=0, tiled=True)  32.7 us
  transfers between devices with their start and end apart: 15, of which 11 were waited for; matrix products, arithmetic and copies ran while one was open for 13% of the time, Pallas kernels for 0%

commit v1 on v0

--- a/solution.py
+++ b/solution.py
@@ -10,6 +10,19 @@
 inv_root_two_pi = 1.0 / math.sqrt(2.0 * math.pi)
 contract_rows = (((0,), (0,)), ((), ()))
 contract_cols = (((1,), (1,)), ((), ()))
+
+
+def ring_gather(x, axis, dim):
+    ways = lax.axis_size(axis)
+    up = [(d, (d + 1) % ways) for d in range(ways)]
+    down = [(d, (d - 1) % ways) for d in range(ways)]
+    earlier, later = ([x], [x])
+    for _ in range(ways // 2):
+        earlier.append(lax.ppermute(earlier[-1], axis, up))
+    for _ in range((ways - 1) // 2):
+        later.append(lax.ppermute(later[-1], axis, down))
+    line = jnp.concatenate([*earlier[::-1], *later[1:]], axis=dim)
+    return jnp.roll(line, (lax.axis_index(axis) - ways // 2) * x.shape[dim], axis=dim)
 
 
 def padded_2(x, sides, width):
@@ -41,7 +54,7 @@
     up_loc = lax.all_to_all(w_up, "rows", 1, 0, tiled=True)
     up_loc = lax.all_gather(up_loc, "dp", axis=0, tiled=True)
     down_loc = lax.all_to_all(w_down, "rows", 0, 1, tiled=True)
-    down_loc = lax.all_gather(down_loc, "dp", axis=1, tiled=True)
+    down_loc = ring_gather(down_loc, "dp", 1)
     cotan = d_out.reshape(cells, width).astype(jnp.float32)
     back = (cotan * layer_scale).astype(jnp.bfloat16)
     back_all = lax.all_gather(back, hid_axes, axis=0, tiled=True)

time: 635 us -> 607 us (0.956)
  waiting for transfers between devices: 429 us -> 382 us
  local copies, waits for them, and re-layouts: 30.5 us -> 42.8 us
    ppermute x0 -> x3, waiting for transfers between devices: none -> 47.4 us  [the longest x2 41.5 us: ring_gather(): earlier.append(lax.ppermute(earlier[-1], axis, up))]
    all_gather x1 -> x0, waiting for transfers between devices: 44.2 us -> none  [body(): down_loc = lax.all_gather(down_loc, 'dp', axis=1, tiled=True)]
    all_gather x1, waiting for transfers between devices: 34.1 us -> 0.01 us  [body(): gathered = lax.all_gather(scaled, hid_axes, axis=0, tiled=True)]
    all_gather x1, waiting for transfers between devices: 17.3 us -> 0.01 us  [body(): up_loc = lax.all_gather(up_loc, 'dp', axis=0, tiled=True)]
    unnamed x101 -> x112, local copies, waits for them, and re-layouts: 3.09 us -> 14.5 us
  transfers between devices with their start and end apart: 15 -> 17, of which waited for: 11 -> 11; matrix products, arithmetic and copies ran while one was open for 13% -> 14% of each run, Pallas kernels for 0% -> 0%
where the time goes in v1:
time: 607 us; the launch traced here: 605 us
  waiting for transfers between devices  382 us (63%)
  blocking collectives  69.8 us (11%)
  local copies, waits for them, and re-layouts  42.8 us (7%)
  matrix products  39.9 us (7%)
  other arithmetic  31.4 us (5%)
  starting transfers between devices  24.5 us (4%)
  between operations  15.2 us (3%)
    psum x1, waiting for transfers between devices, body(): lax.psum((kernel_part, gain_part, scale_part), ('dp', 'fsdp', 'rows'))  112 us
    reduce_scatter x1, waiting for transfers between devices, body(): lax.psum_scatter(down_part, 'dp', scatter_dimension=1, tiled=True)  64.9 us
    reduce_scatter x1, waiting for transfers between devices, body(): lax.psum_scatter(norm_terms, hid_axes, scatter_dimension=0, tiled=True)  58.3 us
    reduce_scatter x1, waiting for transfers between devices, body(): lax.psum_scatter(mlp_terms.astype(jnp.bfloat16), hid_axes, scatter_dimens...  47.1 us
    psum x1, blocking collectives, body(): lax.psum((kernel_part, gain_part, scale_part), ('dp', 'fsdp', 'rows'))  46.1 us
    ppermute x2, waiting for transfers between devices, ring_gather(): earlier.append(lax.ppermute(earlier[-1], axis, up))  41.5 us
    all_gather x1, waiting for transfers between devices, body(): back_all = lax.all_gather(back, hid_axes, axis=0, tiled=True)  32.6 us
    another operation x50, local copies, waits for them, and re-layouts, body(): kernel_part = jnp.stack(kernel_rows).reshape(KS, KS, width)  15.7 us
  transfers between devices with their start and end apart: 17, of which 11 were waited for; matrix products, arithmetic and copies ran while one was open for 14% of the time, Pallas kernels for 0%

profile of v1, /device:TPU:1, one launch (start us, length us, event | category | flops | bytes accessed | tf_op | source)
XLA Modules:
  0.0 605.3 jit_solution(11796747628798982255)
XLA Ops:
  7.2 1.2 copy.35
  8.4 13.0 %all_to_all.76 = bf16[96,4,768]{2,0,1:T(8,128)(2,1)} all-to-all(bf16[96,4,768]{2,0,1:T(8,128)(2,1)S(1)} %bitcast.113), channel_id=1, replica_groups=mesh['dp'=4,'fsdp'=2,'rows'=4] {'rows'}, dimensions={1} | all-to-all | bytes 1179648 | tf_op jit(solution)/shard_map/all_to_all | solution.py:54
  21.5 2.6 collective-permute-start
  24.2 1.9 collective-permute-start.1
  27.9 4.3 collective-permute-done.1
  32.8 9.4 %fusion.110 = (f32[4,32]{1,0:T(4,128)S(1)}, f32[1,4,32,1536]{3,2,1,0:T(8,128)S(1)}) fusion(f32[1536]{0:T(1024)S(1)} %get-tuple-element.106, f32[1536]{0:T(1024)S(1)} %get-tuple-element.107, f32[1536]{0:T(1024)S(1)} %get-tuple-element.60, f32[1536]{0:T(1024)S(1)} %get-tuple-element.61, f32[1,10,32,1536]{3,2,1,0:T(8,128)S(1)} %maximum_convert_fusion, ...), kind=kLoop, calls=%fused_computation.328 | loop fusion | flops 19267456 | bytes 8641024 | tf_op jit(solution)/shard_map/reduce_sum | solution.py:72
  43.7 10.7 %all_to_all.77 = bf16[4,768,96]{1,2,0:T(8,128)(2,1)S(1)} all-to-all(bf16[4,768,96]{1,2,0:T(8,128)(2,1)S(1)} %bitcast.114), channel_id=1, replica_groups=mesh['dp'=4,'fsdp'=2,'rows'=4] {'rows'}, dimensions={0} | all-to-all | bytes 1179648 | tf_op jit(solution)/shard_map/all_to_all | solution.py:56
  54.4 1.7 collective-permute-start.2
  56.1 28.8 %collective-permute-done.2 = bf16[768,384]{0,1:T(8,128)(2,1)} collective-permute-done((bf16[768,384]{0,1:T(8,128)(2,1)S(1)}, bf16[768,384]{0,1:T(8,128)(2,1)}, u32[]{:S(2)}, u32[]{:S(2)}) %collective-permute-start.2) | collective-permute-done | bytes 589856 | tf_op jit(solution)/shard_map/ppermute | solution.py:21
  84.9 3.3 collective-permute-start.4
  88.1 12.7 %collective-permute-done.3 = bf16[768,384]{0,1:T(8,128)(2,1)} collective-permute-done((bf16[768,384]{0,1:T(8,128)(2,1)}, bf16[768,384]{0,1:T(8,128)(2,1)}, u32[]{:S(2)}, u32[]{:S(2)}) %collective-permute-start.3) | collective-permute-done | bytes 589856 | tf_op jit(solution)/shard_map/ppermute | solution.py:21
  100.9 1.9 constant_dynamic-update-slice_fusion.7
  102.8 1.9 constant_dynamic-update-slice_fusion.6
  105.6 5.8 collective-permute-done.4
  111.4 1.9 constant_dynamic-update-slice_fusion.4
  113.4 2.0 constant_dynamic-update-slice_fusion.3
  115.3 1.9 constant_dynamic-update-slice_fusion.2
  118.1 1.9 constant_dynamic-update-slice_fusion
  120.0 7.4 %multiply_convert_fusion = (bf16[1024,768]{1,0:T(8,128)(2,1)}, f32[1024,768]{1,0:T(8,128)}) fusion(bf16[1024,1536]{1,0:T(8,128)(2,1)} %all-gather.4.cloned.1.call-done, bf16[1536,768]{1,0:T(8,128)(2,1)} %all-gather.6.cloned.1.call-done), kind=kOutput, calls=%fused_computation.92 | convolution fusion | flops 2419851264 | bytes 10223616 | tf_op jit(solution)/shard_map/dot_general | solution.py:79
  127.4 6.5 %convolution_convert_fusion = bf16[1024,1536]{1,0:T(8,128)(2,1)} fusion(bf16[1024,768]{1,0:T(8,128)(2,1)} %get-tuple-element.120, bf16[768,3072]{0,1:T(8,128)(2,1)} %constant_dynamic-update-slice_fusion, s32[]{:T(128)S(6)} %select_n.14), kind=kOutput, calls=%fused_computation.85 | convolution fusion | flops 2417491968 | bytes 7077892 | tf_op jit(solution)/shard_map/dot_general | solution.py:81
  134.0 47.1 %reduce-scatter.5.cloned.1.call-done = bf16[128,1536]{1,0:T(8,128)(2,1)} async-done(((bf16[1024,1536]{1,0:T(8,128)(2,1)}), bf16[128,1536]{1,0:T(8,128)(2,1)}) %reduce-scatter.5.cloned.1.call-update) | async-done | bytes 393232 | tf_op jit(solution)/shard_map/reduce_scatter | solution.py:82
  181.2 2.7 fusion.13
  184.1 32.6 %all-gather.8.cloned.1.call-done = bf16[1024,1536]{1,0:T(8,128)(2,1)} async-done(((bf16[128,1536]{1,0:T(8,128)(2,1)}), bf16[1024,1536]{1,0:T(8,128)(2,1)}) %all-gather.8.cloned.1.call-update) | async-done | bytes 3145744 | tf_op jit(solution)/shard_map/all_gather | solution.py:60
  216.8 7.2 %fusion.115 = f32[768,1536]{1,0:T(8,128)} fusion(bf16[1024,768]{1,0:T(8,128)(2,1)} %get-tuple-element.120, bf16[1024,1536]{1,0:T(8,128)(2,1)} %all-gather.8.cloned.1.call-done), kind=kOutput, calls=%fused_computation.333 | convolution fusion | flops 2415919104 | bytes 9437184 | tf_op jit(solution)/shard_map/dot_general | solution.py:88
  224.1 6.9 %fusion.5 = bf16[1024,768]{1,0:T(8,128)(2,1)S(1)} fusion(f32[1024,768]{1,0:T(8,128)} %get-tuple-element.121, bf16[1024,1536]{1,0:T(8,128)(2,1)} %all-gather.8.cloned.1.call-done, bf16[768,3072]{0,1:T(8,128)(2,1)} %constant_dynamic-update-slice_fusion, s32[]{:T(128)S(6)} %select_n.14), kind=kOutput, calls=%fused_computation.91 | convolution fusion | flops 2423783424 | bytes 10223620 | tf_op jit(solution)/shard_map/dot_general | solution.py:89
  231.0 1.2 copy-done.51
  232.2 4.6 fusion.113
  236.8 7.2 %fusion.114 = f32[1536,768]{1,0:T(8,128)} fusion(bf16[1024,1536]{1,0:T(8,128)(2,1)} %all-gather.4.cloned.1.call-done, bf16[1024,768]{1,0:T(8,128)(2,1)} %copy-done.51), kind=kOutput, calls=%fused_computation.332 | convolution fusion | flops 2415919104 | bytes 9437184 | tf_op jit(solution)/shard_map/dot_general | solution.py:93
  244.1 64.9 %reduce-scatter.11.cloned.1.call-done = f32[768,384]{1,0:T(8,128)} async-done(((f32[768,1536]{1,0:T(8,128)}), f32[768,384]{1,0:T(8,128)}) %reduce-scatter.11.cloned.1.call-update) | async-done | bytes 1179664 | tf_op jit(solution)/shard_map/reduce_scatter | solution.py:102
  309.1 2.7 copy.26
  311.7 4.9 all-to-all-start.3
  316.6 58.3 %reduce-scatter.7.cloned.1.call-done = f32[128,1536]{1,0:T(8,128)} async-done(((f32[1024,1536]{1,0:T(8,128)}), f32[128,1536]{1,0:T(8,128)}) %reduce-scatter.7.cloned.1.call-update) | async-done | bytes 786448 | tf_op jit(solution)/shard_map/reduce_scatter | solution.py:99
  374.9 2.0 multiply_reduce_fusion
  376.9 3.6 multiply_reduce_fusion.2
  380.5 2.0 multiply_reduce_fusion.1
  394.8 3.6 collective-permute-start.5
  398.4 1.9 collective-permute-start.6
  400.4 1.1 multiply_reduce_fusion.3
  402.0 4.2 stack.199
  406.9 46.1 %all-reduce.2 = (f32[1536]{0:T(1024)}, f32[1536]{0:T(1024)}) all-reduce(f32[1536]{0:T(1024)} %get-tuple-element.56, f32[1536]{0:T(1024)} %get-tuple-element.113), channel_id=1, replica_groups=mesh['dp'=4,'fsdp'=2,'rows'=4] {'dp','fsdp','rows'}, use_global_device_ids=true, to_apply=%region_59.60 | all-reduce | flops 3072 | bytes 24576 | tf_op jit(solution)/shard_map/psum | solution.py:129
  454.2 9.4 %reduce-scatter.9.cloned.1.call-done = f32[384,768]{1,0:T(8,128)} async-done(((f32[1536,768]{1,0:T(8,128)}), f32[384,768]{1,0:T(8,128)}) %reduce-scatter.9.cloned.1.call-update) | async-done | bytes 1179664 | tf_op jit(solution)/shard_map/reduce_scatter | solution.py:100
  463.6 4.1 all-to-all-start.2
  467.7 8.0 %fusion.101 = bf16[1,4,32,1536]{3,2,1,0:T(8,128)(2,1)} fusion(f32[1,10,32,1536]{3,2,1,0:T(8,128)S(1)} %maximum_convert_fusion.1, bf16[1,4,32,1536]{3,2,1,0:T(8,128)(2,1)S(1)} %copy-done.2, f32[1536]{0:T(1024)} %copy-done.15, f32[1536]{0:T(1024)} %copy-done.16, f32[1536]{0:T(1024)} %copy-done.18, f32[1536]{0:T(1024)} %copy-done.19, f32[1536]{0:T(1024)} %copy-done.20, ...), kind=kLoop, calls=%fused_computation.191 | loop fusion | flops 19660800 | bytes 8562688 | tf_op jit(solution)/shard_map/convert_element_type | solution.py:128
  475.7 2.4 copy.31
  478.1 5.2 all-to-all-done.2
  483.3 1.1 copy.30
  484.4 112.2 %all-reduce.5.cloned.1.call-done = f32[7,7,1536]{2,1,0:T(8,128)} async-done(((f32[7,7,1536]{2,1,0:T(8,128)}), f32[7,7,1536]{2,1,0:T(8,128)}) %all-reduce.5.cloned.1.call-update) | async-done | bytes 301072 | tf_op jit(solution)/shard_map/psum | solution.py:129
  596.7 1.7 copy.44
  (195 shorter events, 19.9 us)
Async XLA Ops:
  7.2 14.3 %copy-start = (bf16[1,4,32,1536]{3,2,1,0:T(8,128)(2,1)S(1)}, bf16[1,4,32,1536]{3,2,1,0:T(8,128)(2,1)}, u32[]{:S(2)}) copy-start(bf16[1,4,32,1536]{3,2,1,0:T(8,128)(2,1)} %param.7) | copy-start | bytes 1179652
  7.2 18.9 %copy-start.4 = (f32[7,7,1536]{2,1,0:T(8,128)S(1)}, f32[7,7,1536]{2,1,0:T(8,128)}, u32[]{:S(2)}) copy-start(f32[7,7,1536]{2,1,0:T(8,128)} %param.8) | copy-start | bytes 903172
  7.2 112.8 %all-gather.6.cloned.1.call-start = ((), (), s32[]{:S(2)}) async-start(), calls=%async_computation.9 | async-start | bytes 2949120 | tf_op jit(solution)/shard_map/all_gather | solution.py:55
  21.4 98.6 %all-gather.4.cloned.1.call-start = ((), (), s32[]{:S(2)}) async-start(), calls=%async_computation.8 | async-start | bytes 3538944 | tf_op jit(solution)/shard_map/all_gather | solution.py:78
  21.5 6.3 %collective-permute-start = (bf16[1,3,32,1536]{3,2,1,0:T(8,128)(2,1)S(1)}, bf16[1,3,32,1536]{3,2,1,0:T(8,128)(2,1)S(1)}, u32[]{:S(2)}, u32[]{:S(2)}) collective-permute-start(bf16[1,3,32,1536]{3,2,1,0:T(8,128)(2,1)S(1)} %get-tuple-element.118), channel_id=1, source_target_pairs={{0,1},{1,2},{2,3},{4,5},{5,6},{6,7},{8,9},{9,10},{10,11},{12,13},{... | collective-permute-start | bytes 884744 | tf_op jit(solution)/shard_map/ppermute | solution.py:35
  24.2 8.0 %collective-permute-start.1 = (bf16[1,3,32,1536]{3,2,1,0:T(8,128)(2,1)S(1)}, bf16[1,3,32,1536]{3,2,1,0:T(8,128)(2,1)S(1)}, u32[]{:S(2)}, u32[]{:S(2)}) collective-permute-start(bf16[1,3,32,1536]{3,2,1,0:T(8,128)(2,1)S(1)} %get-tuple-element.119), channel_id=1, source_target_pairs={{1,0},{2,1},{3,2},{5,4},{6,5},{7,6},{9,8},{10,9},{11,10},{13,12},{... | collective-permute-start | bytes 884744 | tf_op jit(solution)/shard_map/ppermute | solution.py:36
  26.3 6.1 %copy-start.6 = (f32[1536]{0:T(1024)}, f32[1536]{0:T(1024)S(1)}, u32[]{:S(2)}) copy-start(f32[1536]{0:T(1024)S(1)} %get-tuple-element.98) | copy-start | bytes 18436
  26.3 6.1 %copy-start.8 = (f32[1536]{0:T(1024)}, f32[1536]{0:T(1024)S(1)}, u32[]{:S(2)}) copy-start(f32[1536]{0:T(1024)S(1)} %get-tuple-element.99) | copy-start | bytes 18436
  26.3 6.1 %copy-start.9 = (f32[1536]{0:T(1024)}, f32[1536]{0:T(1024)S(1)}, u32[]{:S(2)}) copy-start(f32[1536]{0:T(1024)S(1)} %get-tuple-element.100) | copy-start | bytes 18436
  26.3 6.1 %copy-start.10 = (f32[1536]{0:T(1024)}, f32[1536]{0:T(1024)S(1)}, u32[]{:S(2)}) copy-start(f32[1536]{0:T(1024)S(1)} %get-tuple-element.101) | copy-start | bytes 18436
  26.3 6.1 %copy-start.11 = (f32[1536]{0:T(1024)}, f32[1536]{0:T(1024)S(1)}, u32[]{:S(2)}) copy-start(f32[1536]{0:T(1024)S(1)} %get-tuple-element.102) | copy-start | bytes 18436
  26.3 6.1 %copy-start.12 = (f32[1536]{0:T(1024)}, f32[1536]{0:T(1024)S(1)}, u32[]{:S(2)}) copy-start(f32[1536]{0:T(1024)S(1)} %get-tuple-element.103) | copy-start | bytes 18436
  26.4 6.1 %copy-start.13 = (f32[1536]{0:T(1024)}, f32[1536]{0:T(1024)S(1)}, u32[]{:S(2)}) copy-start(f32[1536]{0:T(1024)S(1)} %get-tuple-element.104) | copy-start | bytes 18436
  26.4 6.1 %copy-start.14 = (f32[1536]{0:T(1024)}, f32[1536]{0:T(1024)S(1)}, u32[]{:S(2)}) copy-start(f32[1536]{0:T(1024)S(1)} %get-tuple-element.105) | copy-start | bytes 18436
  26.4 6.1 %copy-start.15 = (f32[1536]{0:T(1024)}, f32[1536]{0:T(1024)S(1)}, u32[]{:S(2)}) copy-start(f32[1536]{0:T(1024)S(1)} %get-tuple-element.106) | copy-start | bytes 18436
  26.4 6.1 %copy-start.16 = (f32[1536]{0:T(1024)}, f32[1536]{0:T(1024)S(1)}, u32[]{:S(2)}) copy-start(f32[1536]{0:T(1024)S(1)} %get-tuple-element.107) | copy-start | bytes 18436
  26.7 5.7 copy-start.17
  26.7 5.7 copy-start.18
  26.7 5.7 copy-start.19
  26.7 5.7 copy-start.20
  26.8 5.7 copy-start.21
  26.8 5.7 copy-start.22
  26.8 5.7 copy-start.23
  26.8 5.7 copy-start.24
  26.8 5.7 copy-start.25
  26.8 5.7 copy-start.26
  32.7 9.9 %copy-start.5 = (f32[1536]{0:T(1024)S(1)}, f32[1536]{0:T(1024)}, u32[]{:S(2)}) copy-start(f32[1536]{0:T(1024)} %param.9) | copy-start | bytes 18436
  42.3 60.5 %copy-start.46 = (f32[128]{0:T(128)}, f32[128]{0:T(128)S(1)}, u32[]{:S(2)}) copy-start(f32[128]{0:T(128)S(1)} %div.15) | copy-start | bytes 1540
  42.6 60.2 %copy-start.48 = (f32[128]{0:T(128)}, f32[128]{0:T(128)S(1)}, u32[]{:S(2)}) copy-start(f32[128]{0:T(128)S(1)} %rsqrt.12) | copy-start | bytes 1540
  43.6 137.6 %reduce-scatter.5.cloned.1.call-start = ((), (), s32[]{:S(2)}) async-start(), calls=%async_computation.10 | async-start | bytes 3538944 | tf_op jit(solution)/shard_map/reduce_scatter | solution.py:82
  54.4 30.5 %collective-permute-start.2 = (bf16[768,384]{0,1:T(8,128)(2,1)S(1)}, bf16[768,384]{0,1:T(8,128)(2,1)}, u32[]{:S(2)}, u32[]{:S(2)}) collective-permute-start(bf16[768,384]{0,1:T(8,128)(2,1)S(1)} %bitcast.106), channel_id=1, source_target_pairs={{0,8},{8,16},{16,24},{24,0},{1,9},{9,17},{17,25},{25,1},{2,10},{10... | collective-permute-start | bytes 1769480 | tf_op jit(solution)/shard_map/ppermute | solution.py:21
  84.9 16.0 %collective-permute-start.3 = (bf16[768,384]{0,1:T(8,128)(2,1)}, bf16[768,384]{0,1:T(8,128)(2,1)}, u32[]{:S(2)}, u32[]{:S(2)}) collective-permute-start(bf16[768,384]{0,1:T(8,128)(2,1)} %collective-permute-done.2), channel_id=1, source_target_pairs={{0,8},{8,16},{16,24},{24,0},{1,9},{9,17},{17,25},{25,1},{2,10},{10... | collective-permute-start | bytes 1769480 | tf_op jit(solution)/shard_map/ppermute | solution.py:21
  84.9 26.5 %collective-permute-start.4 = (bf16[768,384]{0,1:T(8,128)(2,1)S(1)}, bf16[768,384]{0,1:T(8,128)(2,1)}, u32[]{:S(2)}, u32[]{:S(2)}) collective-permute-start(bf16[768,384]{0,1:T(8,128)(2,1)S(1)} %bitcast.107), channel_id=1, source_target_pairs={{0,24},{8,0},{16,8},{24,16},{1,25},{9,1},{17,9},{25,17},{2,26},{10... | collective-permute-start | bytes 1769480 | tf_op jit(solution)/shard_map/ppermute | solution.py:23
  134.0 47.2 %copy-start.1 = (bf16[1,4,32,1536]{3,2,1,0:T(8,128)(2,1)S(1)}, bf16[1,4,32,1536]{3,2,1,0:T(8,128)(2,1)}, u32[]{:S(2)}) copy-start(bf16[1,4,32,1536]{3,2,1,0:T(8,128)(2,1)} %param.7) | copy-start | bytes 1179652
  134.0 47.2 %copy-start.2 = (bf16[1,4,32,1536]{3,2,1,0:T(8,128)(2,1)S(1)}, bf16[1,4,32,1536]{3,2,1,0:T(8,128)(2,1)}, u32[]{:S(2)}) copy-start(bf16[1,4,32,1536]{3,2,1,0:T(8,128)(2,1)} %param.13) | copy-start | bytes 1179652
  134.0 82.8 %all-gather.8.cloned.1.call-start = ((), (), s32[]{:S(2)}) async-start(), calls=%async_computation.11 | async-start | bytes 3538944 | tf_op jit(solution)/shard_map/all_gather | solution.py:60
  183.9 125.2 %reduce-scatter.11.cloned.1.call-start = ((), (), s32[]{:S(2)}) async-start(), calls=%async_computation.14 | async-start | bytes 5898240 | tf_op jit(solution)/shard_map/reduce_scatter | solution.py:102
  224.0 150.9 %reduce-scatter.7.cloned.1.call-start = ((), (), s32[]{:S(2)}) async-start(), calls=%async_computation.12 | async-start | bytes 7077888 | tf_op jit(solution)/shard_map/reduce_scatter | solution.py:99
  224.1 8.1 %copy-start.50 = (bf16[1536,768]{1,0:T(8,128)(2,1)S(1)}, bf16[1536,768]{1,0:T(8,128)(2,1)}, u32[]{:S(2)}) copy-start(bf16[1536,768]{1,0:T(8,128)(2,1)} %all-gather.6.cloned.1.call-done) | copy-start | bytes 7077892
  236.8 226.8 %reduce-scatter.9.cloned.1.call-start = ((), (), s32[]{:S(2)}) async-start(), calls=%async_computation.13 | async-start | bytes 5898240 | tf_op jit(solution)/shard_map/reduce_scatter | solution.py:100
  244.1 130.8 %copy-start.47 = (f32[128]{0:T(128)S(1)}, f32[128]{0:T(128)}, u32[]{:S(2)}) copy-start(f32[128]{0:T(128)} %copy-done.46) | copy-start | bytes 1540
  244.1 130.8 %copy-start.49 = (f32[128]{0:T(128)S(1)}, f32[128]{0:T(128)}, u32[]{:S(2)}) copy-start(f32[128]{0:T(128)} %copy-done.48) | copy-start | bytes 1540
  311.7 151.8 %all-to-all-start.3 = ((f32[768,4,96]{0,2,1:T(8,128)}), f32[768,4,96]{0,2,1:T(8,128)}, u32[]{:S(2)}, u32[]{:S(2)}) async-start(f32[768,4,96]{0,2,1:T(8,128)} %bitcast.110), calls=%async_computation.7 | async-start | bytes 2359296 | tf_op jit(solution)/shard_map/all_to_all | solution.py:103
  316.6 280.1 %all-reduce.5.cloned.1.call-start = ((), (), s32[]{:S(2)}) async-start(), calls=%async_computation.15 | async-start | bytes 688128 | tf_op jit(solution)/shard_map/psum | solution.py:129
  394.8 58.2 %collective-permute-start.5 = (bf16[1,3,32,1536]{3,2,1,0:T(8,128)(2,1)}, bf16[1,3,32,1536]{3,2,1,0:T(8,128)(2,1)S(1)}, u32[]{:S(2)}, u32[]{:S(2)}) collective-permute-start(bf16[1,3,32,1536]{3,2,1,0:T(8,128)(2,1)} %get-tuple-element.116), channel_id=1, source_target_pairs={{0,1},{1,2},{2,3},{4,5},{5,6},{6,7},{8,9},{9,10},{10,11},{12,13},{... | collective-permute-start | bytes 884744 | tf_op jit(solution)/shard_map/ppermute | solution.py:35
  398.4 54.6 %collective-permute-start.6 = (bf16[1,3,32,1536]{3,2,1,0:T(8,128)(2,1)}, bf16[1,3,32,1536]{3,2,1,0:T(8,128)(2,1)}, u32[]{:S(2)}, u32[]{:S(2)}) collective-permute-start(bf16[1,3,32,1536]{3,2,1,0:T(8,128)(2,1)} %get-tuple-element.117), channel_id=1, source_target_pairs={{1,0},{2,1},{3,2},{5,4},{6,5},{7,6},{9,8},{10,9},{11,10},{13,12},{... | collective-permute-start | bytes 884744 | tf_op jit(solution)/shard_map/ppermute | solution.py:36
  453.0 14.7 %copy-start.7 = (f32[1536]{0:T(1024)S(1)}, f32[1536]{0:T(1024)}, u32[]{:S(2)}) copy-start(f32[1536]{0:T(1024)} %copy-done.6) | copy-start | bytes 18436
  463.6 19.8 %all-to-all-start.2 = ((f32[4,96,768]{2,1,0:T(8,128)}), f32[4,96,768]{2,1,0:T(8,128)S(1)}, u32[]{:S(2)}, u32[]{:S(2)}) async-start(f32[4,96,768]{2,1,0:T(8,128)} %bitcast.116), calls=%async_computation.5 | async-start | bytes 2359296 | tf_op jit(solution)/shard_map/all_to_all | solution.py:101
  (21 other events, 103.0 us)
Sparse Core Ops, SparseCore 0:
  21.5 63.6 all-gather.5
  87.7 31.6 all-gather.3
  134.1 47.0 reduce-scatter.4
  184.0 32.7 all-gather.7
  224.1 84.8 reduce-scatter.10
  312.7 62.1 reduce-scatter.6
  377.2 86.3 reduce-scatter.8
  469.5 127.1 all-reduce.4
